TPU v7x, 256 devices: a whole 4x4x8 slice. The times are simulated.
256 devices in a mesh: lon: 64 (over y, z, x_hi), lat: 4 (over x_lo, core).
Axes of the slice: x: 4 (x_hi: 2, x_lo: 2; x = x_hi * 2 + x_lo), y: 4, z: 8, core: 2. Of those that a mesh axis runs over, the one named last changes fastest.
Arguments:
- initial_state: float32 [4, 32, 1024, 512], P(None, None, 'lon', 'lat'), may hold values from -6 to 6
- coefficients: float32 [4, 32, 1024, 512], P(None, None, 'lon', 'lat'), may hold values from 0.02 to 0.24
- coupling: float32 [32, 4, 4], replicated, may hold values from -3 to 3
- obs_band: int32 [4, 32768, 1], P('lat', 'lon'), may hold values from 0 to 63; in each aligned block of 512 rows (0 to 511, 512 to 1023, ..., all dimensions but the last counted through in order) at most 32 rows name the same one
- obs_cell: int32 [4, 32768], P('lat', 'lon'), may hold values from 0 to 262143
- obs_value: float32 [4, 32768], P('lat', 'lon'), may hold values from -6 to 6
- obs_weight: float32 [4, 32768], P('lat', 'lon'), may hold values from 0.5 to 4
- obs_count: int32 [4, 64], P('lat', 'lon'), may hold values from 256 to 512
Outputs:
- final_state: float32 [4, 32, 1024, 512], P(None, None, 'lon', 'lat')
- gradient: float32 [4, 32, 1024, 512], P(None, None, 'lon', 'lat')
Inputs may be any that keep to these rules, and one draw needn't show every extreme that they name: `obs_band`: in the 512 rows of one device no band is named more than 32 times, a bound that some block reaches.
All inputs are finite; a program needn't handle non-finite values.
Results may differ from a plain program's by a relative error of at most 0.0003.
Values sent between devices are 32-bit elements; how exact they have to be, the bound alone decides.
No kernel may reach another device: no remote copies, remote signals or barrier semaphores. Data moves between devices by JAX's collectives and lax.ppermute only.
A program may use at most 128 MiB of HBM per device.

v0:
```python
import jax
import jax.numpy as jnp
from jax import lax
from jax.sharding import PartitionSpec as P

STEPS = 2


def extended(array, sides, width, wrap):
    for axis, dim in sides:
        peers, length = (lax.axis_size(axis), array.shape[dim])
        up = [(i, (i + 1) % peers) for i in range(peers if wrap else peers - 1)]
        down = [(j, i) for i, j in up]
        last = lax.slice_in_dim(array, length - width, length, axis=dim)
        initial = lax.slice_in_dim(array, 0, width, axis=dim)
        before = lax.ppermute(last, axis, up)
        after = lax.ppermute(initial, axis, down)
        array = jnp.concatenate([before, array, after], axis=dim)
    return array


def passed_along(value, axis, steps):
    count = lax.axis_size(axis)
    pairs = [(source, (source + steps) % count) for source in range(count)]
    return lax.ppermute(value, axis, pairs)


def neighbours(field, flip):
    ext_lon = extended(field, (("lon", 2),), 1, True)
    ext_lat = extended(field, (("lat", 3),), 1, False)
    west = ext_lon[:, :, :-2, :]
    east = ext_lon[:, :, 2:, :]
    north = ext_lat[:, :, :, :-2]
    south = ext_lat[:, :, :, 2:]
    edges = jnp.stack([field[:, :, :, 0], field[:, :, :, -1]])
    partner = passed_along(edges, "lon", lax.axis_size("lon") // 2)
    position = lax.axis_index("lat")
    last_block = lax.axis_size("lat") - 1
    north = north.at[:, :, :, 0].set(jnp.where(position == 0, flip * partner[0], north[:, :, :, 0]))
    south = south.at[:, :, :, -1].set(
        jnp.where(position == last_block, flip * partner[1], south[:, :, :, -1])
    )
    return (north, south, west, east)


def on_device(
    initial_state, coefficients, coupling, obs_band, obs_cell, obs_value, obs_weight, obs_count
):
    wind_flip = jnp.array([-1.0, -1.0, 1.0, 1.0], dtype=jnp.float32).reshape(4, 1, 1)
    plain_flip = jnp.ones((4, 1, 1), jnp.float32)
    total = coefficients[0] + coefficients[1] + coefficients[2] + coefficients[3]
    stored = []
    x = initial_state
    for step in range(STEPS):
        forward_north, forward_south, forward_west, forward_east = neighbours(x, wind_flip)
        mixed = jnp.einsum("lgf,flij->glij", coupling, x, precision=lax.Precision.HIGHEST)
        y = (
            x
            + coefficients[0] * forward_north
            + coefficients[1] * forward_south
            + coefficients[2] * forward_west
            + coefficients[3] * forward_east
            - total * x
            + 0.25 * mixed
        )
        stored.append(y)
        x = y - 0.5 * jnp.tanh(y)
    rows = obs_cell.shape[1]
    band = obs_band[0, :, 0]
    valid = jnp.arange(rows, dtype=jnp.int32) < obs_count[0, 0]
    weight = jnp.where(valid, obs_weight[0], 0.0)
    cell_float = obs_cell[0].astype(jnp.float32)
    payload = jnp.stack([obs_value[0], weight, cell_float, band.astype(jnp.float32)])
    arrived = lax.all_gather(payload, "lon", axis=1, tiled=True)
    owned = (arrived[3] == lax.axis_index("lon").astype(jnp.float32)).astype(jnp.float32)
    values = arrived[0]
    weights = arrived[1] * owned
    cells = arrived[2].astype(jnp.int32)
    flat_state = x.reshape(-1)
    forcing = weights * (flat_state[cells] - values)
    lam = jnp.zeros_like(flat_state).at[cells].add(forcing).reshape(x.shape)
    near_n, near_s, near_w, near_e = neighbours(coefficients, plain_flip)
    row_ids = jnp.arange(coefficients.shape[3], dtype=jnp.int32)[None, :]
    polar_top = (lax.axis_index("lat") == 0) & (row_ids == 0)
    polar_bottom = (lax.axis_index("lat") == lax.axis_size("lat") - 1) & (
        row_ids == coefficients.shape[3] - 1
    )
    from_north = jnp.where(polar_top, near_n[0], near_n[1])
    from_south = jnp.where(polar_bottom, near_s[1], near_s[0])
    from_west = near_w[3]
    from_east = near_e[2]
    for step in range(STEPS - 1, -1, -1):
        squashed = jnp.tanh(stored[step])
        lam_y = lam * (1.0 - 0.5 * (1.0 - squashed * squashed))
        north, south, west, east = neighbours(lam_y, wind_flip)
        back = jnp.einsum("lgf,glij->flij", coupling, lam_y, precision=lax.Precision.HIGHEST)
        lam = (
            lam_y
            - total * lam_y
            + 0.25 * back
            + from_north * north
            + from_south * south
            + from_west * west
            + from_east * east
        )
    return (x, lam)


def solution(mesh):
    in_specs = (
        P(None, None, "lon", "lat"),
        P(None, None, "lon", "lat"),
        P(),
        P("lat", "lon", None),
        P("lat", "lon"),
        P("lat", "lon"),
        P("lat", "lon"),
        P("lat", "lon"),
    )
    out_specs = (P(None, None, "lon", "lat"), P(None, None, "lon", "lat"))
    return jax.shard_map(
        on_device, mesh=mesh, in_specs=in_specs, out_specs=out_specs, check_vma=False
    )
```

profile of v0, /device:TPU:1, one launch (start us, length us, event | category | flops | bytes accessed | tf_op | source)
XLA Modules:
  0.0 978.5 jit_solution(12267966740924993856)
XLA Ops:
  30.8 157.5 %all_gather.3 = f32[4,32768]{1,0:T(4,128)S(1)} all-gather(f32[4,512]{1,0:T(4,128)S(1)} %pad_maximum_fusion.25), channel_id=1, replica_groups=mesh['lon'=64,'lat'=4] {'lon'}, dimensions={1}, use_global_device_ids=true | all-gather | bytes 532480 | tf_op jit(solution)/shard_map/all_gather | solution.py:74
  197.1 4.6 pad_maximum_fusion.17
  206.8 10.1 %collective-permute-start.1 = (f32[2,4,32,16]{2,3,1,0:T(8,128)}, f32[2,4,32,16]{2,3,1,0:T(8,128)}, u32[]{:S(2)}, u32[]{:S(2)}) collective-permute-start(f32[2,4,32,16]{2,3,1,0:T(8,128)} %pad_maximum_fusion.20), channel_id=1, source_target_pairs={{0,128},{4,132},{8,136},{12,140},{16,144},{20,148},{24,152},{28,15... | collective-permute-start | bytes 49160 | tf_op jit(solution)/shard_map/ppermute | solution.py:25
  249.3 4.0 scatter.40
  253.3 3.8 multiply_select_fusion.7
  257.1 12.0 %scatter.44 = f32[4,32,16,128]{3,2,1,0:T(8,128)} dynamic-update-slice(f32[4,32,16,128]{3,2,1,0:T(8,128)} %get-tuple-element.157, f32[4,32,16,1]{3,2,1,0:T(8,128)} %copy.737, s32[]{:T(128)} %constant.234.clone.1, s32[]{:T(128)} %constant.234.clone.1, s32[]{:T(128)} %constant.234.clone.1, s32[]{:T(128)} %constant.236.clone.1) | dynamic-update-slice | bytes 16388 | tf_op jit(solution)/shard_map/scatter | solution.py:40
  271.1 43.3 %scatter.35 = f32[4,32,16,128]{3,0,2,1:T(4,128)} dynamic-update-slice(f32[4,32,16,128]{3,0,2,1:T(4,128)} %get-tuple-element.182, f32[4,32,16,1]{3,0,2,1:T(4,128)S(1)} %copy-done.6, s32[]{:T(128)} %constant.234.clone.1, s32[]{:T(128)} %constant.234.clone.1, s32[]{:T(128)} %constant.234.clone.1, s32[]{:T(128)} %constant.236.clone.1) | dynamic-update-slice | bytes 16388 | tf_op jit(solution)/shard_map/scatter | solution.py:40
  314.4 8.9 scatter.34
  325.3 5.2 multiply_subtract_fusion.3
  331.8 4.3 collective-permute-start.9
  337.4 32.4 %collective-permute-start.5 = (f32[4,32,16,1]{1,2,3,0:T(8,128)}, f32[4,32,16,1]{1,2,3,0:T(8,128)S(1)}, u32[]{:S(2)}, u32[]{:S(2)}) collective-permute-start(f32[4,32,16,1]{1,2,3,0:T(8,128)} %copy.708), channel_id=1, source_target_pairs={{0,1},{1,2},{2,3},{4,5},{5,6},{6,7},{8,9},{9,10},{10,11},{12,13},{... | collective-permute-start | bytes 24584 | tf_op jit(solution)/shard_map/ppermute | solution.py:16
  391.0 43.3 %scatter.39 = f32[4,32,16,128]{3,0,2,1:T(4,128)} dynamic-update-slice(f32[4,32,16,128]{3,0,2,1:T(4,128)} %get-tuple-element.176, f32[4,32,16,1]{3,0,2,1:T(4,128)} %get-tuple-element.204, s32[]{:T(128)} %constant.234.clone.1, s32[]{:T(128)} %constant.234.clone.1, s32[]{:T(128)} %constant.234.clone.1, s32[]{:T(128)} %constant.236.clone.1) | dynamic-update-slice | bytes 16388 | tf_op jit(solution)/shard_map/scatter | solution.py:40
  434.3 8.0 scatter.36
  442.3 5.9 multiply_subtract_fusion.2
  449.2 180.5 %gather_fusion = f32[32768]{0:T(1024)S(1)} fusion(f32[262144]{0:T(1024)S(1)} %bitcast.99, s32[32768]{0:T(1024)S(1)} %copy-done.17), kind=kCustom, calls=%fused_computation | custom fusion | bytes 393216 | tf_op jit(solution)/shard_map/gather | solution.py:80
  629.8 171.5 %scatter_custom_fusion = f32[262144]{0:T(1024)S(1)} fusion(s32[32768]{0:T(1024)S(1)} %bitcast.108, f32[32768]{0:T(1024)S(1)} %subtract_multiply_fusion, f32[]{:T(128)} %constant.239.clone.1), kind=kCustom, calls=%fused_computation.65 | custom fusion | flops 32768 | bytes 1048580 | tf_op jit(solution)/shard_map/scatter-add | solution.py:81
  803.5 8.1 collective-permute-start.19
  832.1 43.3 %scatter.45 = f32[4,32,16,128]{3,0,2,1:T(4,128)} dynamic-update-slice(f32[4,32,16,128]{3,0,2,1:T(4,128)} %get-tuple-element.170, f32[4,32,16,1]{3,0,2,1:T(4,128)} %get-tuple-element.202, s32[]{:T(128)} %constant.234.clone.1, s32[]{:T(128)} %constant.234.clone.1, s32[]{:T(128)} %constant.234.clone.1, s32[]{:T(128)} %constant.236.clone.1) | dynamic-update-slice | bytes 16388 | tf_op jit(solution)/shard_map/scatter | solution.py:40
  875.4 8.0 scatter.41
  883.5 4.9 fusion.12
  889.7 7.5 collective-permute-start.24
  921.1 43.3 %scatter.49 = f32[4,32,16,128]{3,0,2,1:T(4,128)} dynamic-update-slice(f32[4,32,16,128]{3,0,2,1:T(4,128)} %get-tuple-element.151, f32[4,32,16,1]{3,0,2,1:T(4,128)} %get-tuple-element.200, s32[]{:T(128)} %constant.234.clone.1, s32[]{:T(128)} %constant.234.clone.1, s32[]{:T(128)} %constant.234.clone.1, s32[]{:T(128)} %constant.236.clone.1) | dynamic-update-slice | bytes 16388 | tf_op jit(solution)/shard_map/scatter | solution.py:40
  964.5 8.0 scatter.46
  972.5 4.6 fusion.7
  (191 shorter events, 153.2 us)
Async XLA Ops:
  2.6 320.7 %collective-permute-start.16 = (f32[4,32,1,128]{3,2,1,0:T(1,128)}, f32[4,32,1,128]{3,2,1,0:T(1,128)}, u32[]{:S(2)}, u32[]{:S(2)}) collective-permute-start(f32[4,32,1,128]{3,2,1,0:T(1,128)} %get-tuple-element.167), channel_id=1, source_target_pairs={{0,4},{4,8},{8,12},{12,16},{16,20},{20,24},{24,28},{28,32},{32,36}... | collective-permute-start | bytes 196616 | tf_op jit(solution)/shard_map/ppermute | solution.py:16
  9.2 183.9 %collective-permute-start = (f32[4,32,16,1]{1,2,3,0:T(8,128)}, f32[4,32,16,1]{1,2,3,0:T(8,128)}, u32[]{:S(2)}, u32[]{:S(2)}) collective-permute-start(f32[4,32,16,1]{1,2,3,0:T(8,128)} %copy.767), channel_id=1, source_target_pairs={{0,1},{1,2},{2,3},{4,5},{5,6},{6,7},{8,9},{9,10},{10,11},{12,13},{... | collective-permute-start | bytes 24584 | tf_op jit(solution)/shard_map/ppermute | solution.py:16
  13.4 181.7 %collective-permute-start.2 = (f32[4,32,16,1]{1,2,3,0:T(8,128)}, f32[4,32,16,1]{1,2,3,0:T(8,128)}, u32[]{:S(2)}, u32[]{:S(2)}) collective-permute-start(f32[4,32,16,1]{1,2,3,0:T(8,128)} %copy.768), channel_id=1, source_target_pairs={{1,0},{2,1},{3,2},{5,4},{6,5},{7,6},{9,8},{10,9},{11,10},{13,12},{... | collective-permute-start | bytes 24584 | tf_op jit(solution)/shard_map/ppermute | solution.py:17
  19.0 182.6 %collective-permute-start.10 = (f32[4,32,16,1]{1,2,3,0:T(8,128)}, f32[4,32,16,1]{1,2,3,0:T(8,128)}, u32[]{:S(2)}, u32[]{:S(2)}) collective-permute-start(f32[4,32,16,1]{1,2,3,0:T(8,128)} %copy.769), channel_id=1, source_target_pairs={{0,1},{1,2},{2,3},{4,5},{5,6},{6,7},{8,9},{9,10},{10,11},{12,13},{... | collective-permute-start | bytes 24584 | tf_op jit(solution)/shard_map/ppermute | solution.py:16
  23.8 183.0 %collective-permute-start.14 = (f32[4,32,16,1]{1,2,3,0:T(8,128)}, f32[4,32,16,1]{1,2,3,0:T(8,128)}, u32[]{:S(2)}, u32[]{:S(2)}) collective-permute-start(f32[4,32,16,1]{1,2,3,0:T(8,128)} %copy.770), channel_id=1, source_target_pairs={{1,0},{2,1},{3,2},{5,4},{6,5},{7,6},{9,8},{10,9},{11,10},{13,12},{... | collective-permute-start | bytes 24584 | tf_op jit(solution)/shard_map/ppermute | solution.py:17
  193.1 130.2 %collective-permute-start.18 = (f32[4,32,1,128]{3,2,1,0:T(1,128)}, f32[4,32,1,128]{3,2,1,0:T(1,128)}, u32[]{:S(2)}, u32[]{:S(2)}) collective-permute-start(f32[4,32,1,128]{3,2,1,0:T(1,128)} %get-tuple-element.168), channel_id=1, source_target_pairs={{4,0},{8,4},{12,8},{16,12},{20,16},{24,20},{28,24},{32,28},{36,32}... | collective-permute-start | bytes 196616 | tf_op jit(solution)/shard_map/ppermute | solution.py:17
  195.0 130.2 %collective-permute-start.4 = (f32[4,32,1,128]{3,0,2,1:T(4,128)}, f32[4,32,1,128]{3,0,2,1:T(4,128)}, u32[]{:S(2)}, u32[]{:S(2)}) collective-permute-start(f32[4,32,1,128]{3,0,2,1:T(4,128)} %get-tuple-element.186), channel_id=1, source_target_pairs={{4,0},{8,4},{12,8},{16,12},{20,16},{24,20},{28,24},{32,28},{36,32}... | collective-permute-start | bytes 196616 | tf_op jit(solution)/shard_map/ppermute | solution.py:17
  201.6 123.6 %collective-permute-start.3 = (f32[4,32,1,128]{3,0,2,1:T(4,128)}, f32[4,32,1,128]{3,0,2,1:T(4,128)}, u32[]{:S(2)}, u32[]{:S(2)}) collective-permute-start(f32[4,32,1,128]{3,0,2,1:T(4,128)} %get-tuple-element.185), channel_id=1, source_target_pairs={{0,4},{4,8},{8,12},{12,16},{16,20},{20,24},{24,28},{28,32},{32,36}... | collective-permute-start | bytes 196616 | tf_op jit(solution)/shard_map/ppermute | solution.py:16
  206.8 21.3 %collective-permute-start.1 = (f32[2,4,32,16]{2,3,1,0:T(8,128)}, f32[2,4,32,16]{2,3,1,0:T(8,128)}, u32[]{:S(2)}, u32[]{:S(2)}) collective-permute-start(f32[2,4,32,16]{2,3,1,0:T(8,128)} %pad_maximum_fusion.20), channel_id=1, source_target_pairs={{0,128},{4,132},{8,136},{12,140},{16,144},{20,148},{24,152},{28,15... | collective-permute-start | bytes 49160 | tf_op jit(solution)/shard_map/ppermute | solution.py:25
  228.1 9.5 collective-permute-start.11
  331.8 110.5 %collective-permute-start.9 = (f32[4,32,1,128]{3,0,2,1:T(4,128)}, f32[4,32,1,128]{3,0,2,1:T(4,128)}, u32[]{:S(2)}, u32[]{:S(2)}) collective-permute-start(f32[4,32,1,128]{3,0,2,1:T(4,128)} %get-tuple-element.180), channel_id=1, source_target_pairs={{4,0},{8,4},{12,8},{16,12},{20,16},{24,20},{28,24},{32,28},{36,32}... | collective-permute-start | bytes 196616 | tf_op jit(solution)/shard_map/ppermute | solution.py:17
  336.1 106.2 %collective-permute-start.8 = (f32[4,32,1,128]{3,0,2,1:T(4,128)}, f32[4,32,1,128]{3,0,2,1:T(4,128)}, u32[]{:S(2)}, u32[]{:S(2)}) collective-permute-start(f32[4,32,1,128]{3,0,2,1:T(4,128)} %get-tuple-element.179), channel_id=1, source_target_pairs={{0,4},{4,8},{8,12},{12,16},{16,20},{20,24},{24,28},{28,32},{32,36}... | collective-permute-start | bytes 196616 | tf_op jit(solution)/shard_map/ppermute | solution.py:16
  337.4 35.6 %collective-permute-start.5 = (f32[4,32,16,1]{1,2,3,0:T(8,128)}, f32[4,32,16,1]{1,2,3,0:T(8,128)S(1)}, u32[]{:S(2)}, u32[]{:S(2)}) collective-permute-start(f32[4,32,16,1]{1,2,3,0:T(8,128)} %copy.708), channel_id=1, source_target_pairs={{0,1},{1,2},{2,3},{4,5},{5,6},{6,7},{8,9},{9,10},{10,11},{12,13},{... | collective-permute-start | bytes 24584 | tf_op jit(solution)/shard_map/ppermute | solution.py:16
  373.0 7.7 collective-permute-start.6
  803.5 80.0 %collective-permute-start.19 = (f32[4,32,1,128]{3,0,2,1:T(4,128)}, f32[4,32,1,128]{3,0,2,1:T(4,128)}, u32[]{:S(2)}, u32[]{:S(2)}) collective-permute-start(f32[4,32,1,128]{3,0,2,1:T(4,128)} %get-tuple-element.174), channel_id=1, source_target_pairs={{4,0},{8,4},{12,8},{16,12},{20,16},{24,20},{28,24},{32,28},{36,32}... | collective-permute-start | bytes 196616 | tf_op jit(solution)/shard_map/ppermute | solution.py:17
  811.5 71.9 %collective-permute-start.17 = (f32[4,32,1,128]{3,0,2,1:T(4,128)S(1)}, f32[4,32,1,128]{3,0,2,1:T(4,128)}, u32[]{:S(2)}, u32[]{:S(2)}) collective-permute-start(f32[4,32,1,128]{3,0,2,1:T(4,128)S(1)} %get-tuple-element.173), channel_id=1, source_target_pairs={{0,4},{4,8},{8,12},{12,16},{16,20},{20,24},{24,28},{28,32},{32,36}... | collective-permute-start | bytes 196616 | tf_op jit(solution)/shard_map/ppermute | solution.py:16
  812.2 7.1 collective-permute-start.12
  814.8 5.7 collective-permute-start.15
  817.2 7.4 collective-permute-start.13
  889.7 82.7 %collective-permute-start.24 = (f32[4,32,1,128]{3,0,2,1:T(4,128)}, f32[4,32,1,128]{3,0,2,1:T(4,128)}, u32[]{:S(2)}, u32[]{:S(2)}) collective-permute-start(f32[4,32,1,128]{3,0,2,1:T(4,128)} %get-tuple-element.155), channel_id=1, source_target_pairs={{4,0},{8,4},{12,8},{16,12},{20,16},{24,20},{28,24},{32,28},{36,32}... | collective-permute-start | bytes 196616 | tf_op jit(solution)/shard_map/ppermute | solution.py:17
  897.2 75.2 %collective-permute-start.23 = (f32[4,32,1,128]{3,0,2,1:T(4,128)}, f32[4,32,1,128]{3,0,2,1:T(4,128)}, u32[]{:S(2)}, u32[]{:S(2)}) collective-permute-start(f32[4,32,1,128]{3,0,2,1:T(4,128)} %get-tuple-element.154), channel_id=1, source_target_pairs={{0,4},{4,8},{8,12},{12,16},{16,20},{20,24},{24,28},{28,32},{32,36}... | collective-permute-start | bytes 196616 | tf_op jit(solution)/shard_map/ppermute | solution.py:16
  898.1 7.2 collective-permute-start.20
  902.4 5.6 collective-permute-start.22
  904.9 8.0 collective-permute-start.21
  (34 other events, 756.0 us)
where the time goes:
time: 989 us; the launch traced here: 979 us
  local copies, waits for them, and re-layouts  481 us (49%)
  other arithmetic  217 us (22%)
  blocking collectives  158 us (16%)
  starting transfers between devices  96.8 us (10%)
  matrix products  20.6 us (2%)
    scatter x5, local copies, waits for them, and re-layouts, neighbours(): south.at[:, :, :, -1]  185 us
    gather x1, local copies, waits for them, and re-layouts, on_device(): forcing = weights * (flat_state[cells] - values)  181 us
    scatter-add x1, other arithmetic, on_device(): lam = jnp.zeros_like(flat_state).at[cells].add(forcing).reshape(x.shape)  171 us
    all_gather x1, blocking collectives, on_device(): arrived = lax.all_gather(payload, 'lon', axis=1, tiled=True)  158 us
    ppermute x10, starting transfers between devices, extended(): before = lax.ppermute(last, axis, up)  51.3 us
    scatter x5, local copies, waits for them, and re-layouts, neighbours(): north.at[:, :, :, 0]  36.8 us
    ppermute x10, starting transfers between devices, extended(): after = lax.ppermute(initial, axis, down)  30 us
  transfers between devices with their start and end apart: 25, of which 2 were waited for; matrix products, arithmetic and copies ran while one was open for 34% of the time, Pallas kernels for 0%

commit v1 on v0

--- a/solution.py
+++ b/solution.py
@@ -71,7 +71,9 @@
     weight = jnp.where(valid, obs_weight[0], 0.0)
     cell_float = obs_cell[0].astype(jnp.float32)
     payload = jnp.stack([obs_value[0], weight, cell_float, band.astype(jnp.float32)])
-    arrived = lax.all_gather(payload, "lon", axis=1, tiled=True)
+    arrived = jnp.concatenate(
+        lax.all_to_all(jnp.stack([payload] * lax.axis_size("lon")), "lon", 0, 0), axis=1
+    )
     owned = (arrived[3] == lax.axis_index("lon").astype(jnp.float32)).astype(jnp.float32)
     values = arrived[0]
     weights = arrived[1] * owned

time: 989 us -> 811 us (0.82)
  blocking collectives: 158 us -> 0 us
  local copies, waits for them, and re-layouts: 481 us -> 468 us
    all_gather x1 -> x0, blocking collectives: 158 us -> none  [on_device(): arrived = lax.all_gather(payload, 'lon', axis=1, tiled=True)]
    ppermute x10, starting transfers between devices: 51.3 us -> 24 us  [extended(): before = lax.ppermute(last, axis, up)]
    all_to_all x0 -> x1, starting transfers between devices: none -> 14 us  [on_device(): lax.all_to_all(jnp.stack([payload] * lax.axis_size('lon')), 'lon', 0, 0)]
  transfers between devices with their start and end apart: 25 -> 26, of which waited for: 2 -> 2; matrix products, arithmetic and copies ran while one was open for 34% -> 41% of each run, Pallas kernels for 0% -> 0%
where the time goes in v1:
time: 811 us; the launch traced here: 801 us
  local copies, waits for them, and re-layouts  468 us (58%)
  other arithmetic  216 us (27%)
  starting transfers between devices  94.6 us (12%)
  matrix products  19.5 us (2%)
    scatter x5, local copies, waits for them, and re-layouts, neighbours(): south.at[:, :, :, -1]  185 us
    gather x1, local copies, waits for them, and re-layouts, on_device(): forcing = weights * (flat_state[cells] - values)  181 us
    scatter-add x1, other arithmetic, on_device(): lam = jnp.zeros_like(flat_state).at[cells].add(forcing).reshape(x.shape)  171 us
    ppermute x10, starting transfers between devices, extended(): after = lax.ppermute(initial, axis, down)  38.2 us
    scatter x5, local copies, waits for them, and re-layouts, neighbours(): north.at[:, :, :, 0]  36.8 us
    ppermute x10, starting transfers between devices, extended(): before = lax.ppermute(last, axis, up)  24 us
    ppermute x5, starting transfers between devices, passed_along(): return lax.ppermute(value, axis, pairs)  18.4 us
    concatenate x5, other arithmetic, extended(): array = jnp.concatenate([before, array, after], axis=dim)  17.3 us
  transfers between devices with their start and end apart: 26, of which 2 were waited for; matrix products, arithmetic and copies ran while one was open for 41% of the time, Pallas kernels for 0%

profile of v1, /device:TPU:1, one launch (start us, length us, event | category | flops | bytes accessed | tf_op | source)
XLA Modules:
  0.0 801.4 jit_solution(15531496562600123826)
XLA Ops:
  16.0 14.0 %all-to-all-start = ((f32[64,4,512]{2,1,0:T(4,128)}), f32[64,4,512]{2,1,0:T(4,128)}, u32[]{:S(2)}, u32[]{:S(2)}) async-start(f32[64,4,512]{2,1,0:T(4,128)} %stack.17), calls=%async_computation | async-start | bytes 1048576 | tf_op jit(solution)/shard_map/all_to_all | solution.py:75
  42.6 7.9 collective-permute-start.18
  54.4 4.6 pad_maximum_fusion.17
  63.4 11.2 %collective-permute-start.1 = (f32[2,4,32,16]{2,3,1,0:T(8,128)S(1)}, f32[2,4,32,16]{2,3,1,0:T(8,128)S(1)}, u32[]{:S(2)}, u32[]{:S(2)}) collective-permute-start(f32[2,4,32,16]{2,3,1,0:T(8,128)S(1)} %pad_maximum_fusion.20), channel_id=1, source_target_pairs={{0,128},{4,132},{8,136},{12,140},{16,144},{20,148},{24,152},{28,15... | collective-permute-start | bytes 49160 | tf_op jit(solution)/shard_map/ppermute | solution.py:25
  98.6 4.0 scatter.40
  106.4 12.0 %scatter.44 = f32[4,32,16,128]{3,2,1,0:T(8,128)} dynamic-update-slice(f32[4,32,16,128]{3,2,1,0:T(8,128)} %get-tuple-element.157, f32[4,32,16,1]{3,2,1,0:T(8,128)} %copy.737, s32[]{:T(128)} %constant.234.clone.1, s32[]{:T(128)} %constant.234.clone.1, s32[]{:T(128)} %constant.234.clone.1, s32[]{:T(128)} %constant.236.clone.1) | dynamic-update-slice | bytes 16388 | tf_op jit(solution)/shard_map/scatter | solution.py:40
  120.4 43.3 %scatter.35 = f32[4,32,16,128]{3,0,2,1:T(4,128)} dynamic-update-slice(f32[4,32,16,128]{3,0,2,1:T(4,128)} %get-tuple-element.182, f32[4,32,16,1]{3,0,2,1:T(4,128)S(1)} %copy-done.6, s32[]{:T(128)} %constant.234.clone.1, s32[]{:T(128)} %constant.234.clone.1, s32[]{:T(128)} %constant.234.clone.1, s32[]{:T(128)} %constant.236.clone.1) | dynamic-update-slice | bytes 16388 | tf_op jit(solution)/shard_map/scatter | solution.py:40
  163.7 8.9 %scatter.34 = f32[4,32,16,128]{3,0,2,1:T(4,128)} dynamic-update-slice(f32[4,32,16,128]{3,0,2,1:T(4,128)} %get-tuple-element.181, f32[4,32,16,1]{3,0,2,1:T(4,128)S(1)} %copy-done.5, s32[]{:T(128)} %constant.234.clone.1, s32[]{:T(128)} %constant.234.clone.1, s32[]{:T(128)} %constant.234.clone.1, s32[]{:T(128)} %constant.234.clone.1) | dynamic-update-slice | bytes 16388 | tf_op jit(solution)/shard_map/scatter | solution.py:39
  175.2 5.2 multiply_subtract_fusion.3
  181.7 4.3 collective-permute-start.9
  186.7 5.0 collective-permute-start.5
  210.9 43.3 %scatter.39 = f32[4,32,16,128]{3,0,2,1:T(4,128)} dynamic-update-slice(f32[4,32,16,128]{3,0,2,1:T(4,128)} %get-tuple-element.176, f32[4,32,16,1]{3,0,2,1:T(4,128)} %get-tuple-element.205, s32[]{:T(128)} %constant.234.clone.1, s32[]{:T(128)} %constant.234.clone.1, s32[]{:T(128)} %constant.234.clone.1, s32[]{:T(128)} %constant.236.clone.1) | dynamic-update-slice | bytes 16388 | tf_op jit(solution)/shard_map/scatter | solution.py:40
  254.3 8.0 scatter.36
  263.2 4.8 multiply_subtract_fusion.2
  270.7 180.5 %gather_fusion = f32[32768]{0:T(1024)S(1)} fusion(f32[262144]{0:T(1024)S(1)} %bitcast.97, s32[32768]{0:T(1024)S(1)} %broadcast_clamp_fusion), kind=kCustom, calls=%fused_computation | custom fusion | bytes 393216 | tf_op jit(solution)/shard_map/gather | solution.py:82
  451.3 171.5 %scatter_custom_fusion = f32[262144]{0:T(1024)S(1)} fusion(s32[32768]{0:T(1024)S(1)} %bitcast.107, f32[32768]{0:T(1024)S(1)} %subtract_multiply_fusion, f32[]{:T(128)} %constant.239.clone.1), kind=kCustom, calls=%fused_computation.65 | custom fusion | flops 32768 | bytes 1048580 | tf_op jit(solution)/shard_map/scatter-add | solution.py:83
  625.0 8.0 %collective-permute-start.19 = (f32[4,32,1,128]{3,0,2,1:T(4,128)}, f32[4,32,1,128]{3,0,2,1:T(4,128)}, u32[]{:S(2)}, u32[]{:S(2)}) collective-permute-start(f32[4,32,1,128]{3,0,2,1:T(4,128)} %get-tuple-element.174), channel_id=1, source_target_pairs={{4,0},{8,4},{12,8},{16,12},{20,16},{24,20},{28,24},{32,28},{36,32}... | collective-permute-start | bytes 196616 | tf_op jit(solution)/shard_map/ppermute | solution.py:17
  655.3 43.3 %scatter.45 = f32[4,32,16,128]{3,0,2,1:T(4,128)} dynamic-update-slice(f32[4,32,16,128]{3,0,2,1:T(4,128)} %get-tuple-element.170, f32[4,32,16,1]{3,0,2,1:T(4,128)} %get-tuple-element.203, s32[]{:T(128)} %constant.234.clone.1, s32[]{:T(128)} %constant.234.clone.1, s32[]{:T(128)} %constant.234.clone.1, s32[]{:T(128)} %constant.236.clone.1) | dynamic-update-slice | bytes 16388 | tf_op jit(solution)/shard_map/scatter | solution.py:40
  698.6 8.0 scatter.41
  706.6 4.9 fusion.12
  712.9 8.2 %collective-permute-start.24 = (f32[4,32,1,128]{3,0,2,1:T(4,128)}, f32[4,32,1,128]{3,0,2,1:T(4,128)}, u32[]{:S(2)}, u32[]{:S(2)}) collective-permute-start(f32[4,32,1,128]{3,0,2,1:T(4,128)} %get-tuple-element.155), channel_id=1, source_target_pairs={{4,0},{8,4},{12,8},{16,12},{20,16},{24,20},{28,24},{32,28},{36,32}... | collective-permute-start | bytes 196616 | tf_op jit(solution)/shard_map/ppermute | solution.py:17
  744.0 43.3 %scatter.49 = f32[4,32,16,128]{3,0,2,1:T(4,128)} dynamic-update-slice(f32[4,32,16,128]{3,0,2,1:T(4,128)} %get-tuple-element.151, f32[4,32,16,1]{3,0,2,1:T(4,128)} %get-tuple-element.201, s32[]{:T(128)} %constant.234.clone.1, s32[]{:T(128)} %constant.234.clone.1, s32[]{:T(128)} %constant.234.clone.1, s32[]{:T(128)} %constant.236.clone.1) | dynamic-update-slice | bytes 16388 | tf_op jit(solution)/shard_map/scatter | solution.py:40
  787.3 8.0 scatter.46
  795.3 4.6 fusion.7
  (189 shorter events, 142.3 us)
Async XLA Ops:
  2.6 170.0 %collective-permute-start.16 = (f32[4,32,1,128]{3,2,1,0:T(1,128)}, f32[4,32,1,128]{3,2,1,0:T(1,128)S(1)}, u32[]{:S(2)}, u32[]{:S(2)}) collective-permute-start(f32[4,32,1,128]{3,2,1,0:T(1,128)} %get-tuple-element.167), channel_id=1, source_target_pairs={{0,4},{4,8},{8,12},{12,16},{16,20},{20,24},{24,28},{28,32},{32,36}... | collective-permute-start | bytes 196616 | tf_op jit(solution)/shard_map/ppermute | solution.py:16
  8.6 34.0 %collective-permute-start = (f32[4,32,16,1]{1,2,3,0:T(8,128)S(1)}, f32[4,32,16,1]{1,2,3,0:T(8,128)}, u32[]{:S(2)}, u32[]{:S(2)}) collective-permute-start(f32[4,32,16,1]{1,2,3,0:T(8,128)S(1)} %copy.767), channel_id=1, source_target_pairs={{0,1},{1,2},{2,3},{4,5},{5,6},{6,7},{8,9},{9,10},{10,11},{12,13},{... | collective-permute-start | bytes 24584 | tf_op jit(solution)/shard_map/ppermute | solution.py:16
  12.3 40.1 %collective-permute-start.2 = (f32[4,32,16,1]{1,2,3,0:T(8,128)S(1)}, f32[4,32,16,1]{1,2,3,0:T(8,128)}, u32[]{:S(2)}, u32[]{:S(2)}) collective-permute-start(f32[4,32,16,1]{1,2,3,0:T(8,128)S(1)} %copy.768), channel_id=1, source_target_pairs={{1,0},{2,1},{3,2},{5,4},{6,5},{7,6},{9,8},{10,9},{11,10},{13,12},{... | collective-permute-start | bytes 24584 | tf_op jit(solution)/shard_map/ppermute | solution.py:17
  16.0 252.2 %all-to-all-start = ((f32[64,4,512]{2,1,0:T(4,128)}), f32[64,4,512]{2,1,0:T(4,128)}, u32[]{:S(2)}, u32[]{:S(2)}) async-start(f32[64,4,512]{2,1,0:T(4,128)} %stack.17), calls=%async_computation | async-start | bytes 1048576 | tf_op jit(solution)/shard_map/all_to_all | solution.py:75
  33.1 25.9 %collective-permute-start.10 = (f32[4,32,16,1]{1,2,3,0:T(8,128)S(1)}, f32[4,32,16,1]{1,2,3,0:T(8,128)S(1)}, u32[]{:S(2)}, u32[]{:S(2)}) collective-permute-start(f32[4,32,16,1]{1,2,3,0:T(8,128)S(1)} %copy.769), channel_id=1, source_target_pairs={{0,1},{1,2},{2,3},{4,5},{5,6},{6,7},{8,9},{9,10},{10,11},{12,13},{... | collective-permute-start | bytes 24584 | tf_op jit(solution)/shard_map/ppermute | solution.py:16
  36.9 26.5 %collective-permute-start.14 = (f32[4,32,16,1]{1,2,3,0:T(8,128)S(1)}, f32[4,32,16,1]{1,2,3,0:T(8,128)S(1)}, u32[]{:S(2)}, u32[]{:S(2)}) collective-permute-start(f32[4,32,16,1]{1,2,3,0:T(8,128)S(1)} %copy.770), channel_id=1, source_target_pairs={{1,0},{2,1},{3,2},{5,4},{6,5},{7,6},{9,8},{10,9},{11,10},{13,12},{... | collective-permute-start | bytes 24584 | tf_op jit(solution)/shard_map/ppermute | solution.py:17
  42.6 130.6 %collective-permute-start.18 = (f32[4,32,1,128]{3,2,1,0:T(1,128)}, f32[4,32,1,128]{3,2,1,0:T(1,128)}, u32[]{:S(2)}, u32[]{:S(2)}) collective-permute-start(f32[4,32,1,128]{3,2,1,0:T(1,128)} %get-tuple-element.168), channel_id=1, source_target_pairs={{4,0},{8,4},{12,8},{16,12},{20,16},{24,20},{28,24},{32,28},{36,32}... | collective-permute-start | bytes 196616 | tf_op jit(solution)/shard_map/ppermute | solution.py:17
  52.4 122.8 %collective-permute-start.4 = (f32[4,32,1,128]{3,0,2,1:T(4,128)}, f32[4,32,1,128]{3,0,2,1:T(4,128)}, u32[]{:S(2)}, u32[]{:S(2)}) collective-permute-start(f32[4,32,1,128]{3,0,2,1:T(4,128)} %get-tuple-element.186), channel_id=1, source_target_pairs={{4,0},{8,4},{12,8},{16,12},{20,16},{24,20},{28,24},{32,28},{36,32}... | collective-permute-start | bytes 196616 | tf_op jit(solution)/shard_map/ppermute | solution.py:17
  59.0 116.2 %collective-permute-start.3 = (f32[4,32,1,128]{3,0,2,1:T(4,128)}, f32[4,32,1,128]{3,0,2,1:T(4,128)}, u32[]{:S(2)}, u32[]{:S(2)}) collective-permute-start(f32[4,32,1,128]{3,0,2,1:T(4,128)} %get-tuple-element.185), channel_id=1, source_target_pairs={{0,4},{4,8},{8,12},{12,16},{16,20},{20,24},{24,28},{28,32},{32,36}... | collective-permute-start | bytes 196616 | tf_op jit(solution)/shard_map/ppermute | solution.py:16
  63.4 20.1 %collective-permute-start.1 = (f32[2,4,32,16]{2,3,1,0:T(8,128)S(1)}, f32[2,4,32,16]{2,3,1,0:T(8,128)S(1)}, u32[]{:S(2)}, u32[]{:S(2)}) collective-permute-start(f32[2,4,32,16]{2,3,1,0:T(8,128)S(1)} %pad_maximum_fusion.20), channel_id=1, source_target_pairs={{0,128},{4,132},{8,136},{12,140},{16,144},{20,148},{24,152},{28,15... | collective-permute-start | bytes 49160 | tf_op jit(solution)/shard_map/ppermute | solution.py:25
  83.5 6.3 collective-permute-start.11
  181.7 80.5 %collective-permute-start.9 = (f32[4,32,1,128]{3,0,2,1:T(4,128)}, f32[4,32,1,128]{3,0,2,1:T(4,128)}, u32[]{:S(2)}, u32[]{:S(2)}) collective-permute-start(f32[4,32,1,128]{3,0,2,1:T(4,128)} %get-tuple-element.180), channel_id=1, source_target_pairs={{4,0},{8,4},{12,8},{16,12},{20,16},{24,20},{28,24},{32,28},{36,32}... | collective-permute-start | bytes 196616 | tf_op jit(solution)/shard_map/ppermute | solution.py:17
  186.0 77.2 %collective-permute-start.8 = (f32[4,32,1,128]{3,0,2,1:T(4,128)}, f32[4,32,1,128]{3,0,2,1:T(4,128)}, u32[]{:S(2)}, u32[]{:S(2)}) collective-permute-start(f32[4,32,1,128]{3,0,2,1:T(4,128)} %get-tuple-element.179), channel_id=1, source_target_pairs={{0,4},{4,8},{8,12},{12,16},{16,20},{20,24},{24,28},{28,32},{32,36}... | collective-permute-start | bytes 196616 | tf_op jit(solution)/shard_map/ppermute | solution.py:16
  186.7 9.8 %collective-permute-start.5 = (f32[4,32,16,1]{1,2,3,0:T(8,128)S(1)}, f32[4,32,16,1]{1,2,3,0:T(8,128)S(1)}, u32[]{:S(2)}, u32[]{:S(2)}) collective-permute-start(f32[4,32,16,1]{1,2,3,0:T(8,128)S(1)} %copy.708), channel_id=1, source_target_pairs={{0,1},{1,2},{2,3},{4,5},{5,6},{6,7},{8,9},{9,10},{10,11},{12,13},{... | collective-permute-start | bytes 24584 | tf_op jit(solution)/shard_map/ppermute | solution.py:16
  194.9 7.8 collective-permute-start.6
  625.0 81.6 %collective-permute-start.19 = (f32[4,32,1,128]{3,0,2,1:T(4,128)}, f32[4,32,1,128]{3,0,2,1:T(4,128)}, u32[]{:S(2)}, u32[]{:S(2)}) collective-permute-start(f32[4,32,1,128]{3,0,2,1:T(4,128)} %get-tuple-element.174), channel_id=1, source_target_pairs={{4,0},{8,4},{12,8},{16,12},{20,16},{24,20},{28,24},{32,28},{36,32}... | collective-permute-start | bytes 196616 | tf_op jit(solution)/shard_map/ppermute | solution.py:17
  633.0 73.6 %collective-permute-start.17 = (f32[4,32,1,128]{3,0,2,1:T(4,128)}, f32[4,32,1,128]{3,0,2,1:T(4,128)}, u32[]{:S(2)}, u32[]{:S(2)}) collective-permute-start(f32[4,32,1,128]{3,0,2,1:T(4,128)} %get-tuple-element.173), channel_id=1, source_target_pairs={{0,4},{4,8},{8,12},{12,16},{16,20},{20,24},{24,28},{28,32},{32,36}... | collective-permute-start | bytes 196616 | tf_op jit(solution)/shard_map/ppermute | solution.py:16
  633.7 8.0 collective-permute-start.12
  637.4 5.5 collective-permute-start.15
  639.9 7.8 collective-permute-start.13
  712.9 82.4 %collective-permute-start.24 = (f32[4,32,1,128]{3,0,2,1:T(4,128)}, f32[4,32,1,128]{3,0,2,1:T(4,128)}, u32[]{:S(2)}, u32[]{:S(2)}) collective-permute-start(f32[4,32,1,128]{3,0,2,1:T(4,128)} %get-tuple-element.155), channel_id=1, source_target_pairs={{4,0},{8,4},{12,8},{16,12},{20,16},{24,20},{28,24},{32,28},{36,32}... | collective-permute-start | bytes 196616 | tf_op jit(solution)/shard_map/ppermute | solution.py:17
  721.0 74.3 %collective-permute-start.23 = (f32[4,32,1,128]{3,0,2,1:T(4,128)}, f32[4,32,1,128]{3,0,2,1:T(4,128)}, u32[]{:S(2)}, u32[]{:S(2)}) collective-permute-start(f32[4,32,1,128]{3,0,2,1:T(4,128)} %get-tuple-element.154), channel_id=1, source_target_pairs={{0,4},{4,8},{8,12},{12,16},{16,20},{20,24},{24,28},{28,32},{32,36}... | collective-permute-start | bytes 196616 | tf_op jit(solution)/shard_map/ppermute | solution.py:16
  721.9 7.4 collective-permute-start.20
  728.1 7.7 collective-permute-start.21
  (33 other events, 600.4 us)
